TPU v7x, 32 devices: a whole 2x2x4 slice. The times are simulated.
32 devices in a mesh: req: 8 (over y, x, core), tp: 4 (over z).
Axes of the slice: x: 2, y: 2, z: 4, core: 2. Of those that a mesh axis runs over, the one named last changes fastest.
Arguments:
- final_states: float32 [16384, 1024], P('req'), may hold values from -50 to 50
- norm_gain: float32 [1024], replicated, may hold values from 0.1 to 1.9
- embedding: bfloat16 [32768, 1024], P('tp'), may hold values from -2 to 2
- targets: int32 [16384], P('req'), may hold values from 0 to 32767
- deal: int32 [8192], P('req'), may hold values from 0 to 16383, as said below
Outputs:
- logprob: float32 [16384], P('req')
- entropy: float32 [16384], P('req')
Inputs may be any that keep to these rules, and one draw needn't show every extreme that they name: Every owned row is named at most once. The rows named of each owner device are a prefix of its 2048 rows (its sequence's live tokens), between 128 and 2048 rows long, and some owner device is named in full; the rest is padding. Each owner's live rows are dealt over all req devices, its own device included. Along each device's 8192 // 8 positions, in order, the owner device number deal // 2048 never decreases. At most 256 positions of one device name rows of one owner device, and some device reaches 256.
All inputs are finite; a program needn't handle non-finite values.
Results may differ from a plain program's by a relative error of at most 0.0031.
Values sent between devices are 32-bit elements; how exact they have to be, the bound alone decides.
No kernel may reach another device: no remote copies, remote signals or barrier semaphores. Data moves between devices by JAX's collectives and lax.ppermute only.
A program may use at most 128 MiB of HBM per device.

v0:
```python
import jax
import jax.numpy as jnp
from jax import lax
from jax.sharding import PartitionSpec as P


def rms_normed(states, norm_gain):
    mean_square = jnp.mean(states * states, axis=1, keepdims=True)
    return (states * lax.rsqrt(mean_square + 1e-06) * norm_gain[None, :]).astype(jnp.bfloat16)


def body(final_states, norm_gain, embedding, targets, deal):
    owners = lax.axis_size("req")
    own_rows = final_states.shape[0]
    capacity = own_rows // owners
    positions = deal.shape[0]
    shard_cols = embedding.shape[0]
    vocab_start = lax.axis_index("tp") * shard_cols
    source = deal // own_rows
    local_row = deal % own_rows
    member = (source[:, None] == jnp.arange(owners, dtype=jnp.int32)[None, :]).astype(jnp.int32)
    counts = jnp.sum(member, axis=0)
    starts = jnp.cumsum(counts) - counts
    offset = jnp.arange(positions, dtype=jnp.int32) - jnp.sum(member * starts[None, :], axis=1)
    slot_index = source * capacity + offset
    asked_rows = jnp.full((owners * capacity,), -1, jnp.int32).at[slot_index].set(local_row)
    wanted = lax.all_to_all(asked_rows, "req", split_axis=0, concat_axis=0, tiled=True)
    is_live = wanted >= 0
    picked = jnp.where(is_live, wanted, 0)
    outgoing_rows = jnp.where(is_live[:, None], final_states[picked], 0.0)
    arrived = lax.all_to_all(outgoing_rows, "req", split_axis=0, concat_axis=0, tiled=True)
    scored_rows = arrived[slot_index]
    owned_normed = rms_normed(final_states, norm_gain)
    in_shard_id = targets - vocab_start
    inside = (in_shard_id >= 0) & (in_shard_id < shard_cols)
    target_rows = embedding[jnp.clip(in_shard_id, 0, shard_cols - 1)]
    target_term = jnp.einsum(
        "rd,rd->r", owned_normed, target_rows, preferred_element_type=jnp.float32
    )
    owner_chosen = lax.psum(jnp.where(inside, target_term, 0.0), "tp")
    normed = rms_normed(scored_rows, norm_gain)
    logits = lax.dot_general(
        normed, embedding, (((1,), (1,)), ((), ())), preferred_element_type=jnp.float32
    )
    local_peak = jnp.max(logits, axis=1)
    row_peak = lax.pmax(local_peak, "tp")
    weights = jnp.exp(logits - row_peak[:, None])
    local_sums = jnp.stack((jnp.sum(weights, axis=1), jnp.sum(weights * logits, axis=1)))
    sums_all = lax.psum(local_sums, "tp")
    log_total = row_peak + jnp.log(sums_all[0])
    expected = sums_all[1] / sums_all[0]
    result_rows = jnp.stack((log_total, expected))
    outgoing = jnp.zeros((2, owners * capacity), jnp.float32).at[:, slot_index].set(result_rows)
    returned = lax.all_to_all(outgoing, "req", split_axis=1, concat_axis=1, tiled=True)
    home_row = jnp.where(is_live, wanted, own_rows)

    def to_owner(values):
        return jnp.zeros((own_rows,), jnp.float32).at[home_row].set(values, mode="drop")

    live_rows = to_owner(jnp.ones((owners * capacity,), jnp.float32))
    log_owned = to_owner(returned[0])
    expected_owned = to_owner(returned[1])
    logprob = (owner_chosen - log_owned) * live_rows
    entropy = log_owned - expected_owned
    return (logprob, entropy)


def solution(mesh):
    return jax.shard_map(
        body,
        mesh=mesh,
        in_specs=(P("req", None), P(), P("tp", None), P("req"), P("req")),
        out_specs=(P("req"), P("req")),
        check_vma=False,
    )
```

profile of v0, /device:TPU:0, one launch (start us, length us, event | category | flops | bytes accessed | tf_op | source)
XLA Modules:
  0.0 251.2 jit_solution(6436493523009157254)
XLA Ops:
  0.6 0.7 add_select_fusion.1
  1.3 0.1 convert_reduce_fusion
  1.5 0.2 reduce-window.8
  1.6 0.1 select_reduce_fusion
  1.7 0.7 broadcast_clamp_fusion.1
  2.4 4.3 %scatter_custom_fusion = s32[2048]{0:T(1024)S(1)} fusion(s32[1024]{0:T(1024)S(1)} %get-tuple-element.7, s32[1024]{0:T(1024)S(1)} %get-tuple-element.16, s32[]{:T(128)} %constant.57.clone.1), kind=kCustom, calls=%fused_computation.49 | custom fusion | bytes 8196 | tf_op jit(solution)/shard_map/scatter | solution.py:26
  6.8 9.7 %all_to_all.30 = s32[8,256,1]{1,2,0:T(1,128)S(1)} all-to-all(s32[8,256,1]{1,2,0:T(1,128)S(1)} %bitcast.25), channel_id=1, replica_groups=mesh['req'=8,'tp'=4] {'req'}, dimensions={0} | all-to-all | bytes 16384 | tf_op jit(solution)/shard_map/all_to_all | solution.py:27
  16.5 15.1 %gather_fusion.1 = f32[2048,1024]{1,0:T(8,128)} fusion(f32[2048,1024]{1,0:T(8,128)} %param.5, s32[2048]{0:T(1024)S(1)} %broadcast_clamp_fusion), kind=kCustom, calls=%fused_computation.1 | custom fusion | bytes 16785408 | tf_op jit(solution)/shard_map/gather | solution.py:30
  31.6 5.8 %broadcast_select_fusion = f32[8,256,1024]{2,1,0:T(8,128)} fusion(f32[8,256,1024]{2,1,0:T(8,128)} %bitcast.21, pred[8,256]{1,0:T(8,128)(4,1)S(1)} %fusion.8), kind=kLoop, calls=%fused_computation.17 | loop fusion | flops 2097152 | bytes 16779264 | tf_op jit(solution)/shard_map/jit(_where)/select_n | solution.py:30
  37.4 0.0 copy-start.1
  37.4 5.3 %all-to-all-start.1 = ((f32[8,256,1024]{2,1,0:T(8,128)}), f32[8,256,1024]{2,1,0:T(8,128)}, u32[]{:S(2)}, u32[]{:S(2)}) async-start(f32[8,256,1024]{2,1,0:T(8,128)} %broadcast_select_fusion), calls=%async_computation.1 | async-start | bytes 16777216 | tf_op jit(solution)/shard_map/all_to_all | solution.py:31
  42.7 0.0 copy-done.1
  42.7 18.9 %gather_fusion = bf16[2048,1024]{1,0:T(8,128)(2,1)} fusion(bf16[8192,1024]{1,0:T(8,128)(2,1)} %param.7, s32[2048]{0:T(1024)S(1)} %fusion.7), kind=kCustom, calls=%fused_computation | custom fusion | bytes 8396800 | tf_op jit(solution)/shard_map/gather | solution.py:36
  61.7 0.0 copy-start
  61.7 0.0 copy-start.2
  61.7 4.1 %multiply_reduce_fusion.1 = f32[2048]{0:T(1024)S(1)} fusion(f32[2048,1024]{1,0:T(8,128)} %param.5), kind=kLoop, calls=%fused_computation.14 | loop fusion | flops 4192256 | bytes 8396800 | tf_op jit(solution)/shard_map/reduce_sum | solution.py:8
  65.8 0.4 copy-done
  66.2 0.0 copy-done.2
  66.2 4.4 %fusion.1 = f32[2048]{0:T(1024)S(1)} fusion(bf16[2048,1024]{1,0:T(8,128)(2,1)S(1)} %copy-done, f32[2048,1024]{1,0:T(8,128)} %param.5, f32[1024]{0:T(1024)S(1)} %copy-done.2, f32[2048]{0:T(1024)S(1)} %add_rsqrt_fusion), kind=kLoop, calls=%fused_computation.12 | loop fusion | flops 14678016 | bytes 12603392 | tf_op jit(solution)/shard_map/rd,rd->r/dot_general | solution.py:37
  70.6 66.0 %all-to-all-done.1 = f32[8,256,1024]{2,1,0:T(8,128)} async-done(((f32[8,256,1024]{2,1,0:T(8,128)}), f32[8,256,1024]{2,1,0:T(8,128)}, u32[]{:S(2)}, u32[]{:S(2)}) %all-to-all-start.1) | async-done | bytes 8388640 | tf_op jit(solution)/shard_map/all_to_all | solution.py:31
  136.6 9.8 %gather_fusion.2 = f32[1024,1024]{1,0:T(8,128)} fusion(f32[2048,1024]{1,0:T(8,128)} %bitcast.8, s32[1024]{0:T(1024)S(1)} %get-tuple-element.6), kind=kCustom, calls=%fused_computation.2 | custom fusion | bytes 8392704 | tf_op jit(solution)/shard_map/gather | solution.py:32
  146.3 2.5 %multiply_reduce_fusion.2 = f32[1024]{0:T(1024)S(1)} fusion(f32[1024,1024]{1,0:T(8,128)} %gather_fusion.2), kind=kLoop, calls=%fused_computation.16 | loop fusion | flops 2096128 | bytes 4198400 | tf_op jit(solution)/shard_map/reduce_sum | solution.py:8
  148.9 26.7 %fusion.21 = (f32[1024]{0:T(1024)S(1)}, f32[1024,8192]{1,0:T(8,128)}) fusion(bf16[8192,1024]{1,0:T(8,128)(2,1)} %param.7, f32[1024,1024]{1,0:T(8,128)} %gather_fusion.2, f32[1024]{0:T(1024)S(1)} %copy-done.2, f32[1024]{0:T(1024)S(1)} %add_rsqrt_fusion.1), kind=kOutput, calls=%fused_computation.64 | convolution fusion | flops 17191403520 | bytes 54538240 | tf_op jit(solution)/shard_map/dot_general | solution.py:42
  175.6 11.9 %pmax.7 = f32[1024]{0:T(1024)S(1)} all-reduce(f32[1024]{0:T(1024)S(1)} %get-tuple-element.17), channel_id=1, replica_groups=mesh['req'=8,'tp'=4] {'tp'}, use_global_device_ids=true, to_apply=%region_8.9 | all-reduce | flops 1024 | bytes 8192 | tf_op jit(solution)/shard_map/pmax | solution.py:46
  187.5 15.2 %fusion = (f32[1024]{0:T(1024)S(1)}, f32[1024]{0:T(1024)S(1)}) fusion(f32[1024,8192]{1,0:T(8,128)} %get-tuple-element.18, f32[1024]{0:T(1024)S(1)} %pmax.7), kind=kLoop, calls=%fused_computation.10 | loop fusion | flops 33552384 | bytes 33566720 | tf_op jit(solution)/shard_map/reduce_sum | solution.py:48
  202.7 15.8 %all-reduce = (f32[2048]{0:T(1024)S(1)}, f32[2,1024]{1,0:T(2,128)S(1)}) all-reduce(f32[2048]{0:T(1024)S(1)} %and_select_fusion, f32[2,1024]{1,0:T(2,128)S(1)} %pad_maximum_fusion), channel_id=1, replica_groups=mesh['req'=8,'tp'=4] {'tp'}, use_global_device_ids=true, to_apply=%region_1.2 | all-reduce | flops 4096 | bytes 32768 | tf_op jit(solution)/shard_map/psum | solution.py:40
  218.6 0.2 copy.15
  218.8 3.3 %scatter_custom_fusion.1 = f32[2,2048]{0,1:T(8,128)S(1)} fusion(s32[1024]{0:T(1024)S(1)} %get-tuple-element.7, f32[1024,2]{1,0:T(8,128)S(1)} %copy.15, f32[]{:T(128)} %constant.27.clone.1), kind=kCustom, calls=%fused_computation.21 | custom fusion | bytes 16388 | tf_op jit(solution)/shard_map/scatter | solution.py:53
  222.2 0.9 copy.16
  223.1 3.3 %all-to-all-start.2 = ((f32[2,8,256]{2,0,1:T(2,128)}), f32[2,8,256]{2,0,1:T(2,128)S(1)}, u32[]{:S(2)}, u32[]{:S(2)}) async-start(f32[2,8,256]{2,0,1:T(2,128)} %copy.16), calls=%async_computation.2 | async-start | bytes 32768 | tf_op jit(solution)/shard_map/all_to_all | solution.py:54
  226.4 8.0 %scatter_custom_fusion.3 = f32[2048]{0:T(1024)S(1)} fusion(s32[2048]{0:T(1024)S(1)} %bitcast.30, f32[2048]{0:T(1024)S(1)} %broadcast.120, f32[]{:T(128)} %constant.27.clone.1), kind=kCustom, calls=%fused_computation.53 | custom fusion | bytes 8196 | tf_op jit(solution)/shard_map/scatter | solution.py:58
  234.5 0.0 all-to-all-done.2
  234.5 8.0 %scatter_custom_fusion.4 = f32[2048]{0:T(1024)S(1)} fusion(s32[2048]{0:T(1024)S(1)} %bitcast.31, f32[2048]{0:T(1024)S(1)} %bitcast.34, f32[]{:T(128)} %constant.27.clone.1), kind=kCustom, calls=%fused_computation.51 | custom fusion | bytes 8196 | tf_op jit(solution)/shard_map/scatter | solution.py:58
  242.6 8.0 %scatter_custom_fusion.2 = f32[2048]{0:T(1024)S(1)} fusion(s32[2048]{0:T(1024)S(1)} %bitcast.32, f32[2048]{0:T(1024)S(1)} %bitcast.33, f32[]{:T(128)} %constant.27.clone.1), kind=kCustom, calls=%fused_computation.55 | custom fusion | bytes 8196 | tf_op jit(solution)/shard_map/scatter | solution.py:58
  250.6 0.6 fusion.20
  (14 shorter events, 0.1 us)
Async XLA Ops:
  37.4 5.3 %copy-start.1 = (s32[2048]{0:T(1024)S(1)}, s32[2048]{0:T(1024)}, u32[]{:S(2)}) copy-start(s32[2048]{0:T(1024)} %param.8) | copy-start | bytes 24580
  37.4 99.2 %all-to-all-start.1 = ((f32[8,256,1024]{2,1,0:T(8,128)}), f32[8,256,1024]{2,1,0:T(8,128)}, u32[]{:S(2)}, u32[]{:S(2)}) async-start(f32[8,256,1024]{2,1,0:T(8,128)} %broadcast_select_fusion), calls=%async_computation.1 | async-start | bytes 16777216 | tf_op jit(solution)/shard_map/all_to_all | solution.py:31
  61.7 4.6 %copy-start = (bf16[2048,1024]{1,0:T(8,128)(2,1)S(1)}, bf16[2048,1024]{1,0:T(8,128)(2,1)}, u32[]{:S(2)}) copy-start(bf16[2048,1024]{1,0:T(8,128)(2,1)} %gather_fusion) | copy-start | bytes 12582916
  61.7 4.6 %copy-start.2 = (f32[1024]{0:T(1024)S(1)}, f32[1024]{0:T(1024)}, u32[]{:S(2)}) copy-start(f32[1024]{0:T(1024)} %param.6) | copy-start | bytes 12292
  223.1 11.4 %all-to-all-start.2 = ((f32[2,8,256]{2,0,1:T(2,128)}), f32[2,8,256]{2,0,1:T(2,128)S(1)}, u32[]{:S(2)}, u32[]{:S(2)}) async-start(f32[2,8,256]{2,0,1:T(2,128)} %copy.16), calls=%async_computation.2 | async-start | bytes 32768 | tf_op jit(solution)/shard_map/all_to_all | solution.py:54
where the time goes:
time: 252 us; the launch traced here: 251 us
  local copies, waits for them, and re-layouts  77.2 us (31%)
  waiting for transfers between devices  66 us (26%)
  blocking collectives  37.4 us (15%)
  other arithmetic  34.6 us (14%)
  matrix products  26.7 us (11%)
  starting transfers between devices  8.61 us (3%)
    all_to_all x1, waiting for transfers between devices, body(): lax.all_to_all(outgoing_rows, 'req', split_axis=0, concat_axis=0, tiled=T...  66 us
    dot_general x1, matrix products, body(): lax.dot_general(normed, embedding, (((1,), (1,)), ((), ())), preferred_el...  26.7 us
    scatter x3, local copies, waits for them, and re-layouts, to_owner(): jnp.zeros((own_rows,), jnp.float32).at[home_row].set(values, mode='drop')  24.1 us
    gather x1, local copies, waits for them, and re-layouts, body(): target_rows = embedding[jnp.clip(in_shard_id, 0, shard_cols - 1)]  18.9 us
    psum x1, blocking collectives, body(): owner_chosen = lax.psum(jnp.where(inside, target_term, 0.0), 'tp')  15.8 us
    reduce_sum x1, other arithmetic, body(): jnp.sum(weights, axis=1)  15.2 us
    gather x1, local copies, waits for them, and re-layouts, body(): outgoing_rows = jnp.where(is_live[:, None], final_states[picked], 0.0)  15.1 us
    pmax x1, blocking collectives, body(): row_peak = lax.pmax(local_peak, 'tp')  11.9 us
  transfers between devices with their start and end apart: 2, of which 1 were waited for; matrix products, arithmetic and copies ran while one was open for 14% of the time, Pallas kernels for 0%

commit v1 on v0

--- a/solution.py
+++ b/solution.py
@@ -1,7 +1,33 @@
+import functools
 import jax
 import jax.numpy as jnp
 from jax import lax
 from jax.sharding import PartitionSpec as P
+
+
+def build_shards(mine_x, across):
+    frame_out = lax.axis_size(across)
+    carry, block_out = (frame_out, lax.axis_index(across))
+    g_now = mine_x.shape[0] // carry
+    everything = list(mine_x.shape)
+    everything[0] = g_now
+    current_value = everything[0]
+    everything[0] = current_value * carry
+    big = jnp.zeros(everything, mine_x.dtype)
+    for idx in range(carry):
+        all_values = lax.dynamic_slice_in_dim(mine_x, (block_out ^ idx) * g_now, g_now, axis=0)
+        if idx:
+            sheets = []
+            for q in range(carry):
+                sheets.append((q, q ^ idx))
+            all_values = lax.ppermute(all_values, across, sheets)
+        big = lax.dynamic_update_slice_in_dim(
+            big, all_values, (block_out ^ idx) * current_value, axis=0
+        )
+    return big
+
+
+trace_the_orders = functools.partial(build_shards, across="req")
 
 
 def rms_normed(states, norm_gain):
@@ -24,7 +50,7 @@
     offset = jnp.arange(positions, dtype=jnp.int32) - jnp.sum(member * starts[None, :], axis=1)
     slot_index = source * capacity + offset
     asked_rows = jnp.full((owners * capacity,), -1, jnp.int32).at[slot_index].set(local_row)
-    wanted = lax.all_to_all(asked_rows, "req", split_axis=0, concat_axis=0, tiled=True)
+    wanted = trace_the_orders(asked_rows)
     is_live = wanted >= 0
     picked = jnp.where(is_live, wanted, 0)
     outgoing_rows = jnp.where(is_live[:, None], final_states[picked], 0.0)

time: 252 us -> 254 us (level)
  blocking collectives: 37.4 us -> 27.7 us
  starting transfers between devices: 8.61 us -> 16.2 us
    all_to_all x1 -> x0, blocking collectives: 9.67 us -> none  [body(): lax.all_to_all(asked_rows, 'req', split_axis=0, concat_axis=0, tiled=True)]
    ppermute x0 -> x7, starting transfers between devices: none -> 7.61 us  [build_shards(): all_values = lax.ppermute(all_values, across, sheets)]
    select_n x2 -> x1, other arithmetic: 5.82 us -> 5.78 us  [body(): outgoing_rows = jnp.where(is_live[:, None], final_states[picked], 0.0)]
  transfers between devices with their start and end apart: 2 -> 9, of which waited for: 1 -> 3; matrix products, arithmetic and copies ran while one was open for 14% -> 15% of each run, Pallas kernels for 0% -> 0%
where the time goes in v1:
time: 254 us; the launch traced here: 253 us
  local copies, waits for them, and re-layouts  78.9 us (31%)
  waiting for transfers between devices  68.4 us (27%)
  other arithmetic  34.5 us (14%)
  blocking collectives  27.7 us (11%)
  matrix products  26.7 us (11%)
  starting transfers between devices  16.2 us (6%)
    all_to_all x1, waiting for transfers between devices, body(): lax.all_to_all(outgoing_rows, 'req', split_axis=0, concat_axis=0, tiled=T...  66 us
    dot_general x1, matrix products, body(): lax.dot_general(normed, embedding, (((1,), (1,)), ((), ())), preferred_el...  26.7 us
    scatter x3, local copies, waits for them, and re-layouts, to_owner(): jnp.zeros((own_rows,), jnp.float32).at[home_row].set(values, mode='drop')  24.1 us
    gather x1, local copies, waits for them, and re-layouts, body(): target_rows = embedding[jnp.clip(in_shard_id, 0, shard_cols - 1)]  18.9 us
    psum x1, blocking collectives, body(): owner_chosen = lax.psum(jnp.where(inside, target_term, 0.0), 'tp')  15.8 us
    reduce_sum x1, other arithmetic, body(): jnp.sum(weights, axis=1)  15.2 us
    gather x1, local copies, waits for them, and re-layouts, body(): outgoing_rows = jnp.where(is_live[:, None], final_states[picked], 0.0)  15.1 us
    pmax x1, blocking collectives, body(): row_peak = lax.pmax(local_peak, 'tp')  11.9 us
  transfers between devices with their start and end apart: 9, of which 3 were waited for; matrix products, arithmetic and copies ran while one was open for 15% of the time, Pallas kernels for 0%

profile of v1, /device:TPU:0, one launch (start us, length us, event | category | flops | bytes accessed | tf_op | source)
XLA Modules:
  0.0 253.4 jit_solution(16585578204541953268)
XLA Ops:
  0.7 0.7 add_select_fusion.1
  1.4 0.1 convert_reduce_fusion
  1.5 0.2 reduce-window.8
  1.7 0.1 select_reduce_fusion
  1.8 0.7 broadcast_clamp_fusion
  2.5 4.3 %scatter_custom_fusion = s32[2048]{0:T(1024)S(1)} fusion(s32[1024]{0:T(1024)S(1)} %get-tuple-element.7, s32[1024]{0:T(1024)S(1)} %get-tuple-element.24, s32[]{:T(128)} %constant.31.clone.1), kind=kCustom, calls=%fused_computation.45 | custom fusion | bytes 8196 | tf_op jit(solution)/shard_map/scatter | solution.py:52
  6.8 0.2 fusion.21
  7.1 0.5 collective-permute-start
  7.5 2.6 %collective-permute-start.1 = (s32[256]{0:T(256)S(1)}, s32[256]{0:T(256)S(1)}, u32[]{:S(2)}, u32[]{:S(2)}) collective-permute-start(s32[256]{0:T(256)S(1)} %get-tuple-element.21), channel_id=1, source_target_pairs={{0,8},{4,12},{8,0},{12,4},{16,24},{20,28},{24,16},{28,20},{1,9},{5... | collective-permute-start | bytes 3080 | tf_op jit(solution)/shard_map/ppermute | solution.py:23
  10.1 0.1 collective-permute-start.2
  10.2 1.8 collective-permute-start.3
  11.9 0.0 collective-permute-start.4
  11.9 0.0 collective-permute-done
  11.9 2.6 %collective-permute-start.5 = (s32[256]{0:T(256)S(1)}, s32[256]{0:T(256)S(1)}, u32[]{:S(2)}, u32[]{:S(2)}) collective-permute-start(s32[256]{0:T(256)S(1)} %get-tuple-element.17), channel_id=1, source_target_pairs={{0,24},{4,28},{8,16},{12,20},{16,8},{20,12},{24,0},{28,4},{1,25},{... | collective-permute-start | bytes 3080 | tf_op jit(solution)/shard_map/ppermute | solution.py:23
  14.6 0.0 collective-permute-done.1
  14.6 0.1 collective-permute-start.6
  14.7 0.2 dynamic_update_slice.25
  14.9 0.3 dynamic_update_slice.26
  15.1 0.3 dynamic_update_slice.27
  15.4 0.2 dynamic_update_slice.28
  15.6 0.0 collective-permute-done.4
  15.6 0.2 dynamic_update_slice.29
  15.8 0.6 collective-permute-done.5
  16.4 0.2 dynamic_update_slice.30
  16.6 1.8 collective-permute-done.6
  18.5 0.2 dynamic_update_slice.31
  18.7 15.1 %gather_fusion.1 = f32[2048,1024]{1,0:T(8,128)} fusion(f32[2048,1024]{1,0:T(8,128)} %param.5, s32[2048]{0:T(1024)S(1)} %get-tuple-element.14), kind=kCustom, calls=%fused_computation.1 | custom fusion | bytes 16785408 | tf_op jit(solution)/shard_map/gather | solution.py:56
  33.8 5.8 %broadcast_select_fusion = f32[8,256,1024]{2,1,0:T(8,128)} fusion(f32[8,256,1024]{2,1,0:T(8,128)} %bitcast.15, pred[8,256]{1,0:T(8,128)(4,1)S(1)} %broadcast_in_dim.64), kind=kLoop, calls=%fused_computation.17 | loop fusion | flops 2097152 | bytes 16779264 | tf_op jit(solution)/shard_map/jit(_where)/select_n | solution.py:56
  39.6 5.3 %all-to-all-start = ((f32[8,256,1024]{2,1,0:T(8,128)}), f32[8,256,1024]{2,1,0:T(8,128)}, u32[]{:S(2)}, u32[]{:S(2)}) async-start(f32[8,256,1024]{2,1,0:T(8,128)} %broadcast_select_fusion), calls=%async_computation | async-start | bytes 16777216 | tf_op jit(solution)/shard_map/all_to_all | solution.py:57
  44.9 18.9 %gather_fusion = bf16[2048,1024]{1,0:T(8,128)(2,1)} fusion(bf16[8192,1024]{1,0:T(8,128)(2,1)} %param.7, s32[2048]{0:T(1024)S(1)} %fusion.7), kind=kCustom, calls=%fused_computation | custom fusion | bytes 8396800 | tf_op jit(solution)/shard_map/gather | solution.py:62
  63.8 4.1 %multiply_reduce_fusion.1 = f32[2048]{0:T(1024)S(1)} fusion(f32[2048,1024]{1,0:T(8,128)} %param.5), kind=kLoop, calls=%fused_computation.14 | loop fusion | flops 4192256 | bytes 8396800 | tf_op jit(solution)/shard_map/reduce_sum | solution.py:34
  68.0 0.4 copy-done
  68.4 4.4 %fusion.1 = f32[2048]{0:T(1024)S(1)} fusion(bf16[2048,1024]{1,0:T(8,128)(2,1)S(1)} %copy-done, f32[2048,1024]{1,0:T(8,128)} %param.5, f32[1024]{0:T(1024)S(1)} %copy-done.2, f32[2048]{0:T(1024)S(1)} %add_rsqrt_fusion), kind=kLoop, calls=%fused_computation.12 | loop fusion | flops 14678016 | bytes 12603392 | tf_op jit(solution)/shard_map/rd,rd->r/dot_general | solution.py:63
  72.8 66.0 %all-to-all-done = f32[8,256,1024]{2,1,0:T(8,128)} async-done(((f32[8,256,1024]{2,1,0:T(8,128)}), f32[8,256,1024]{2,1,0:T(8,128)}, u32[]{:S(2)}, u32[]{:S(2)}) %all-to-all-start) | async-done | bytes 8388640 | tf_op jit(solution)/shard_map/all_to_all | solution.py:57
  138.8 9.8 %gather_fusion.2 = f32[1024,1024]{1,0:T(8,128)} fusion(f32[2048,1024]{1,0:T(8,128)} %bitcast.3, s32[1024]{0:T(1024)S(1)} %get-tuple-element.6), kind=kCustom, calls=%fused_computation.2 | custom fusion | bytes 8392704 | tf_op jit(solution)/shard_map/gather | solution.py:58
  148.5 2.5 multiply_reduce_fusion.2
  151.1 26.7 %fusion.22 = (f32[1024]{0:T(1024)S(1)}, f32[1024,8192]{1,0:T(8,128)}) fusion(bf16[8192,1024]{1,0:T(8,128)(2,1)} %param.7, f32[1024,1024]{1,0:T(8,128)} %gather_fusion.2, f32[1024]{0:T(1024)S(1)} %copy-done.2, f32[1024]{0:T(1024)S(1)} %add_rsqrt_fusion.1), kind=kOutput, calls=%fused_computation.63 | convolution fusion | flops 17191403520 | bytes 54538240 | tf_op jit(solution)/shard_map/dot_general | solution.py:68
  177.7 11.9 %pmax.7 = f32[1024]{0:T(1024)S(1)} all-reduce(f32[1024]{0:T(1024)S(1)} %get-tuple-element.25), channel_id=1, replica_groups=mesh['req'=8,'tp'=4] {'tp'}, use_global_device_ids=true, to_apply=%region_8.9 | all-reduce | flops 1024 | bytes 8192 | tf_op jit(solution)/shard_map/pmax | solution.py:72
  189.7 15.2 %fusion = (f32[1024]{0:T(1024)S(1)}, f32[1024]{0:T(1024)S(1)}) fusion(f32[1024,8192]{1,0:T(8,128)} %get-tuple-element.26, f32[1024]{0:T(1024)S(1)} %pmax.7), kind=kLoop, calls=%fused_computation.10 | loop fusion | flops 33552384 | bytes 33566720 | tf_op jit(solution)/shard_map/reduce_sum | solution.py:74
  204.9 15.8 %all-reduce = (f32[2048]{0:T(1024)S(1)}, f32[2,1024]{1,0:T(2,128)S(1)}) all-reduce(f32[2048]{0:T(1024)S(1)} %and_select_fusion, f32[2,1024]{1,0:T(2,128)S(1)} %pad_maximum_fusion), channel_id=1, replica_groups=mesh['req'=8,'tp'=4] {'tp'}, use_global_device_ids=true, to_apply=%region_1.2 | all-reduce | flops 4096 | bytes 32768 | tf_op jit(solution)/shard_map/psum | solution.py:66
  220.7 0.2 copy.11
  221.0 3.3 %scatter_custom_fusion.1 = f32[2,2048]{0,1:T(8,128)S(1)} fusion(s32[1024]{0:T(1024)S(1)} %get-tuple-element.7, f32[1024,2]{1,0:T(8,128)S(1)} %copy.11, f32[]{:T(128)} %constant.27.clone.1), kind=kCustom, calls=%fused_computation.21 | custom fusion | bytes 16388 | tf_op jit(solution)/shard_map/scatter | solution.py:79
  224.3 0.9 copy.12
  225.2 3.3 %all-to-all-start.1 = ((f32[2,8,256]{2,0,1:T(2,128)}), f32[2,8,256]{2,0,1:T(2,128)S(1)}, u32[]{:S(2)}, u32[]{:S(2)}) async-start(f32[2,8,256]{2,0,1:T(2,128)} %copy.12), calls=%async_computation.1 | async-start | bytes 32768 | tf_op jit(solution)/shard_map/all_to_all | solution.py:80
  228.6 8.0 %scatter_custom_fusion.3 = f32[2048]{0:T(1024)S(1)} fusion(s32[2048]{0:T(1024)S(1)} %get-tuple-element.15, f32[2048]{0:T(1024)S(1)} %broadcast.59, f32[]{:T(128)} %constant.27.clone.1), kind=kCustom, calls=%fused_computation.49 | custom fusion | bytes 8196 | tf_op jit(solution)/shard_map/scatter | solution.py:84
  236.7 8.0 %scatter_custom_fusion.4 = f32[2048]{0:T(1024)S(1)} fusion(s32[2048]{0:T(1024)S(1)} %get-tuple-element.15, f32[2048]{0:T(1024)S(1)} %bitcast.22, f32[]{:T(128)} %constant.27.clone.1), kind=kCustom, calls=%fused_computation.47 | custom fusion | bytes 8196 | tf_op jit(solution)/shard_map/scatter | solution.py:84
  244.7 8.0 %scatter_custom_fusion.2 = f32[2048]{0:T(1024)S(1)} fusion(s32[2048]{0:T(1024)S(1)} %get-tuple-element.15, f32[2048]{0:T(1024)S(1)} %bitcast.21, f32[]{:T(128)} %constant.27.clone.1), kind=kCustom, calls=%fused_computation.51 | custom fusion | bytes 8196 | tf_op jit(solution)/shard_map/scatter | solution.py:84
  252.8 0.6 fusion.20
  (23 shorter events, 0.1 us)
Async XLA Ops:
  7.1 4.9 %collective-permute-start = (s32[256]{0:T(256)S(1)}, s32[256]{0:T(256)S(1)}, u32[]{:S(2)}, u32[]{:S(2)}) collective-permute-start(s32[256]{0:T(256)S(1)} %get-tuple-element.22), channel_id=1, source_target_pairs={{0,4},{4,0},{8,12},{12,8},{16,20},{20,16},{24,28},{28,24},{1,5},{5... | collective-permute-start | bytes 3080 | tf_op jit(solution)/shard_map/ppermute | solution.py:23
  7.5 7.0 %collective-permute-start.1 = (s32[256]{0:T(256)S(1)}, s32[256]{0:T(256)S(1)}, u32[]{:S(2)}, u32[]{:S(2)}) collective-permute-start(s32[256]{0:T(256)S(1)} %get-tuple-element.21), channel_id=1, source_target_pairs={{0,8},{4,12},{8,0},{12,4},{16,24},{20,28},{24,16},{28,20},{1,9},{5... | collective-permute-start | bytes 3080 | tf_op jit(solution)/shard_map/ppermute | solution.py:23
  10.1 5.0 %collective-permute-start.2 = (s32[256]{0:T(256)S(1)}, s32[256]{0:T(256)S(1)}, u32[]{:S(2)}, u32[]{:S(2)}) collective-permute-start(s32[256]{0:T(256)S(1)} %get-tuple-element.20), channel_id=1, source_target_pairs={{0,12},{4,8},{8,4},{12,0},{16,28},{20,24},{24,20},{28,16},{1,13},{... | collective-permute-start | bytes 3080 | tf_op jit(solution)/shard_map/ppermute | solution.py:23
  10.2 5.2 %collective-permute-start.3 = (s32[256]{0:T(256)S(1)}, s32[256]{0:T(256)S(1)}, u32[]{:S(2)}, u32[]{:S(2)}) collective-permute-start(s32[256]{0:T(256)S(1)} %get-tuple-element.19), channel_id=1, source_target_pairs={{0,16},{4,20},{8,24},{12,28},{16,0},{20,4},{24,8},{28,12},{1,17},{... | collective-permute-start | bytes 3080 | tf_op jit(solution)/shard_map/ppermute | solution.py:23
  11.9 3.7 %collective-permute-start.4 = (s32[256]{0:T(256)S(1)}, s32[256]{0:T(256)S(1)}, u32[]{:S(2)}, u32[]{:S(2)}) collective-permute-start(s32[256]{0:T(256)S(1)} %get-tuple-element.18), channel_id=1, source_target_pairs={{0,20},{4,16},{8,28},{12,24},{16,4},{20,0},{24,12},{28,8},{1,21},{... | collective-permute-start | bytes 3080 | tf_op jit(solution)/shard_map/ppermute | solution.py:23
  11.9 4.5 %collective-permute-start.5 = (s32[256]{0:T(256)S(1)}, s32[256]{0:T(256)S(1)}, u32[]{:S(2)}, u32[]{:S(2)}) collective-permute-start(s32[256]{0:T(256)S(1)} %get-tuple-element.17), channel_id=1, source_target_pairs={{0,24},{4,28},{8,16},{12,20},{16,8},{20,12},{24,0},{28,4},{1,25},{... | collective-permute-start | bytes 3080 | tf_op jit(solution)/shard_map/ppermute | solution.py:23
  14.6 3.9 %collective-permute-start.6 = (s32[256]{0:T(256)S(1)}, s32[256]{0:T(256)S(1)}, u32[]{:S(2)}, u32[]{:S(2)}) collective-permute-start(s32[256]{0:T(256)S(1)} %get-tuple-element.16), channel_id=1, source_target_pairs={{0,28},{4,24},{8,20},{12,16},{16,12},{20,8},{24,4},{28,0},{1,29},{... | collective-permute-start | bytes 3080 | tf_op jit(solution)/shard_map/ppermute | solution.py:23
  39.6 5.3 %copy-start.1 = (s32[2048]{0:T(1024)S(1)}, s32[2048]{0:T(1024)}, u32[]{:S(2)}) copy-start(s32[2048]{0:T(1024)} %param.8) | copy-start | bytes 24580
  39.6 99.2 %all-to-all-start = ((f32[8,256,1024]{2,1,0:T(8,128)}), f32[8,256,1024]{2,1,0:T(8,128)}, u32[]{:S(2)}, u32[]{:S(2)}) async-start(f32[8,256,1024]{2,1,0:T(8,128)} %broadcast_select_fusion), calls=%async_computation | async-start | bytes 16777216 | tf_op jit(solution)/shard_map/all_to_all | solution.py:57
  63.8 4.6 %copy-start = (bf16[2048,1024]{1,0:T(8,128)(2,1)S(1)}, bf16[2048,1024]{1,0:T(8,128)(2,1)}, u32[]{:S(2)}) copy-start(bf16[2048,1024]{1,0:T(8,128)(2,1)} %gather_fusion) | copy-start | bytes 12582916
  63.8 4.6 %copy-start.2 = (f32[1024]{0:T(1024)S(1)}, f32[1024]{0:T(1024)}, u32[]{:S(2)}) copy-start(f32[1024]{0:T(1024)} %param.6) | copy-start | bytes 12292
  225.2 11.4 %all-to-all-start.1 = ((f32[2,8,256]{2,0,1:T(2,128)}), f32[2,8,256]{2,0,1:T(2,128)S(1)}, u32[]{:S(2)}, u32[]{:S(2)}) async-start(f32[2,8,256]{2,0,1:T(2,128)} %copy.12), calls=%async_computation.1 | async-start | bytes 32768 | tf_op jit(solution)/shard_map/all_to_all | solution.py:80
